TPU v7x, 256 devices: a whole 4x4x8 slice. The times are simulated.
256 devices in a mesh: tm: 64 (over z, x, core), wafer: 4 (over y).
Axes of the slice: x: 4, y: 4, z: 8, core: 2. Of those that a mesh axis runs over, the one named last changes fastest.
Arguments:
- timestream: bfloat16 [1024, 262144], P('wafer', 'tm'), may hold values from -6 to 6
- sample_weight: bfloat16 [1024, 262144], P('wafer', 'tm'), may hold values from 0 to 4
- response: float32 [3, 1024], replicated, may hold values from -1 to 1
- band_filter: bfloat16 [256, 256], replicated, may hold values from -0.375 to 0.375
- whiten: bfloat16 [7, 1024, 1024], P(None, ('tm', 'wafer')), as said below
- group_wafer: int32 [64], replicated, may hold values from 0 to 6
- pointing: bfloat16 [1024, 6, 256, 256], P(('tm', 'wafer')), may hold values from -0.15625 to 0.15625
- tile_list: int32 [1024, 6], P(('tm', 'wafer')), may hold values from 0 to 2047, as said below
- tile_home: int32 [2048], replicated, may hold values from 0 to 2047, as said below
- solution: float32 [2048, 3, 256], P('tm'), may hold values from -6 to 6
- direction: float32 [2048, 3, 256], P('tm'), may hold values from -6 to 6
- cg_scalars: float32 [2], replicated, may hold values from 0.5 to 1.5
Outputs:
- solution_next: float32 [2048, 3, 256], P('tm')
- residual_next: float32 [2048, 3, 256], P('tm')
- direction_next: float32 [2048, 3, 256], P('tm')
Inputs may be any that keep to these rules, and one draw needn't show every extreme that they name: `tile_list`: the tiles named in the spans of one device (one index of tm and one of wafer) are all different; among them at most 2 have their row tile_home on one index of tm, and in every draw, for each index of wafer, some index of tm owns exactly 2 tiles named by every device of that wafer index. A permutation: row tile_home[i] of a map holds sky tile i. `whiten`: each whitening matrix is symmetric.
All inputs are finite; a program needn't handle non-finite values.
Results may differ from a plain program's by a relative error of at most 0.0033.
The roundings to bfloat16 on the way count: a program that leaves them out, or rounds other values in their place, can miss the bound.
Values may be sent and summed in bfloat16 or wider, within the bound.
No kernel may reach another device: no remote copies, remote signals or barrier semaphores. Data moves between devices by JAX's collectives and lax.ppermute only.
A program may use at most 128 MiB of HBM per device.

v0:
```python
import jax
import jax.numpy as jnp
from jax import lax
from jax.sharding import PartitionSpec as P


def shards(
    timestream,
    sample_weight,
    response,
    band_filter,
    whiten,
    group_wafer,
    pointing,
    tile_list,
    tile_home,
    solution,
    direction,
    cg_scalars,
):
    precise_mode = lax.Precision.HIGHEST
    tm_count = lax.axis_size("tm")
    tm_index = lax.axis_index("tm")
    step_size = cg_scalars[0]
    blend_weight = cg_scalars[1]
    updated = solution + step_size * direction
    short_map = updated.astype(jnp.bfloat16)
    tiles_own, comp_count, pixel_count = solution.shape
    spans_here, per_span = tile_list.shape
    samples = band_filter.shape[0]
    det_total = whiten.shape[2]
    row_count = spans_here * per_span
    capacity = max(2, (row_count + tm_count - 1) // tm_count)
    tile_ids = tile_list.reshape(row_count)
    home_rows = jnp.take(tile_home, tile_ids, axis=0)
    owners = home_rows // tiles_own
    local_slot = home_rows % tiles_own
    positions = jnp.arange(row_count, dtype=jnp.int32)
    earlier = (owners[:, None] == owners[None, :]) & (positions[None, :] < positions[:, None])
    before_count = jnp.sum(earlier.astype(jnp.int32), axis=1)
    targets = owners * capacity + before_count
    placing = targets[:, None] == jnp.arange(tm_count * capacity, dtype=jnp.int32)[None, :]
    requests = jnp.sum(jnp.where(placing, local_slot[:, None], 0), axis=0)
    requests = requests.reshape(tm_count, capacity)
    asked_slots = lax.all_to_all(requests, "tm", split_axis=0, concat_axis=0, tiled=True)
    served = jnp.take(short_map, asked_slots, axis=0)
    replies, asked_slots = (
        lax.all_to_all(served, "tm", split_axis=0, concat_axis=0, tiled=True),
        asked_slots,
    )
    fetched = jnp.take(
        replies.reshape(tm_count * capacity, comp_count, pixel_count), targets, axis=0
    )
    fetched = fetched.reshape(spans_here, per_span, comp_count, pixel_count)
    signal_parts = jnp.einsum(
        "cktp,ckjp->cjt", pointing, fetched, preferred_element_type=jnp.float32
    )
    wafer_pick = group_wafer[tm_index]
    matrix = lax.dynamic_index_in_dim(
        lax.all_gather(whiten, ("tm", "wafer"), axis=1, tiled=True), wafer_pick, 0, keepdims=False
    )
    columns, column_weights = (
        lax.all_to_all(timestream, "wafer", split_axis=1, concat_axis=0, tiled=True),
        lax.all_to_all(sample_weight, "wafer", split_axis=1, concat_axis=0, tiled=True),
    )
    column_weights = column_weights.astype(jnp.float32).reshape(det_total, spans_here, samples)
    signal = jnp.einsum("jd,cjt->dct", response, signal_parts, precision=precise_mode)
    errors = (
        (columns.astype(jnp.float32).reshape(det_total, spans_here, samples) - signal)
        * column_weights
    ).astype(jnp.bfloat16)
    filtered = jnp.dot(
        errors.reshape(det_total * spans_here, samples),
        band_filter,
        preferred_element_type=jnp.float32,
    )
    filtered = filtered.astype(jnp.bfloat16).reshape(det_total, spans_here * samples)
    whitened = jnp.dot(matrix, filtered, preferred_element_type=jnp.float32).astype(jnp.bfloat16)
    smoothed = lax.dot_general(
        whitened.reshape(det_total * spans_here, samples),
        band_filter,
        (((1,), (1,)), ((), ())),
        preferred_element_type=jnp.float32,
    )
    smoothed = smoothed.astype(jnp.bfloat16).reshape(det_total, spans_here, samples)
    stokes = jnp.einsum(
        "jd,dct->cjt",
        response,
        smoothed.astype(jnp.float32) * column_weights,
        precision=precise_mode,
    )
    stokes_short = stokes.astype(jnp.bfloat16)
    partial_value = jnp.einsum(
        "cjt,cktp->ckjp", stokes_short, pointing, preferred_element_type=jnp.float32
    )
    partial_value = partial_value.reshape(row_count, comp_count * pixel_count)
    outgoing = jnp.dot(placing.astype(jnp.float32).T, partial_value, precision=precise_mode)
    outgoing = outgoing.reshape(tm_count, capacity, comp_count, pixel_count)
    arrived = lax.all_to_all(outgoing, "tm", split_axis=0, concat_axis=0, tiled=True)
    slot_hits = (
        asked_slots.reshape(-1)[None, :] == jnp.arange(tiles_own, dtype=jnp.int32)[:, None]
    ).astype(jnp.float32)
    owned_sum = jnp.dot(
        slot_hits,
        arrived.reshape(tm_count * capacity, comp_count * pixel_count),
        precision=precise_mode,
    )
    owned_sum = owned_sum.reshape(tiles_own, comp_count, pixel_count)
    summed = lax.psum(owned_sum, "wafer")
    residual_next = summed * float(det_total) ** (-0.5)
    direction_next = residual_next + blend_weight * direction
    return (updated, residual_next, direction_next)


def solution(mesh):
    in_specs = (
        P("wafer", "tm"),
        P("wafer", "tm"),
        P(),
        P(),
        P(None, ("tm", "wafer"), None),
        P(),
        P(("tm", "wafer"), None, None, None),
        P(("tm", "wafer"), None),
        P(),
        P("tm", None, None),
        P("tm", None, None),
        P(),
    )
    out_specs = (P("tm", None, None), P("tm", None, None), P("tm", None, None))
    return jax.shard_map(shards, mesh=mesh, in_specs=in_specs, out_specs=out_specs, check_vma=False)
```

profile of v0, /device:TPU:2, one launch (start us, length us, event | category | flops | bytes accessed | tf_op | source)
XLA Modules:
  0.0 281.9 jit_solution(5731134282750877064)
XLA Ops:
  7.2 1.6 copy.111
  8.9 0.8 reshape.319
  9.6 0.8 reshape.318
  10.4 1.4 gather_fusion
  11.8 0.2 convert_reduce_fusion
  12.0 0.1 select_reduce_fusion
  12.1 0.8 all_to_all.36
  12.9 12.0 %all-to-all-start = ((s32[64,1,2]{2,1,0:T(1,128)}), s32[64,1,2]{2,1,0:T(1,128)S(1)}, u32[]{:S(2)}, u32[]{:S(2)}) async-start(s32[64,1,2]{2,1,0:T(1,128)} %bitcast.2), calls=%async_computation | async-start | bytes 65536 | tf_op jit(solution)/shard_map/all_to_all | solution.py:45
  24.9 1.4 fusion.34
  26.3 2.4 fusion.33
  28.7 4.8 %all-to-all-done = s32[64,1,2]{2,1,0:T(1,128)S(1)} async-done(((s32[64,1,2]{2,1,0:T(1,128)}), s32[64,1,2]{2,1,0:T(1,128)S(1)}, u32[]{:S(2)}, u32[]{:S(2)}) %all-to-all-start) | async-done | bytes 544 | tf_op jit(solution)/shard_map/all_to_all | solution.py:45
  33.5 0.1 copy.116
  33.7 0.1 copy.118
  33.8 0.1 reshape.339
  33.9 0.1 copy-done.3
  34.1 0.8 gather_fusion.1
  34.9 0.9 broadcast_select_fusion
  35.9 5.5 %all-to-all-start.2 = ((bf16[64,2,3,256]{3,1,2,0:T(2,128)(2,1)}), bf16[64,2,3,256]{3,1,2,0:T(2,128)(2,1)S(1)}, u32[]{:S(2)}, u32[]{:S(2)}) async-start(bf16[64,2,3,256]{3,1,2,0:T(2,128)(2,1)} %broadcast_select_fusion), calls=%async_computation.2 | async-start | bytes 393216 | tf_op jit(solution)/shard_map/all_to_all | solution.py:48
  41.4 4.1 %copy.113 = bf16[256,4096]{0,1:T(8,128)(2,1)} copy(bf16[256,4096]{1,0:T(8,128)(2,1)} %param.12) | data formatting | bytes 4194304 | tf_op args[0]
  45.5 7.3 %all-to-all-done.2 = bf16[64,2,3,256]{3,1,2,0:T(2,128)(2,1)S(1)} async-done(((bf16[64,2,3,256]{3,1,2,0:T(2,128)(2,1)}), bf16[64,2,3,256]{3,1,2,0:T(2,128)(2,1)S(1)}, u32[]{:S(2)}, u32[]{:S(2)}) %all-to-all-start.2) | async-done | bytes 196640 | tf_op jit(solution)/shard_map/all_to_all | solution.py:48
  52.7 4.5 %all-to-all-start.1 = ((bf16[256,4,1024]{0,2,1:T(8,128)(2,1)}), bf16[256,4,1024]{0,2,1:T(8,128)(2,1)}, u32[]{:S(2)}, u32[]{:S(2)}) async-start(bf16[256,4,1024]{0,2,1:T(8,128)(2,1)} %bitcast.99), calls=%async_computation.1 | async-start | bytes 4194304 | tf_op jit(solution)/shard_map/all_to_all | solution.py:63
  57.2 4.1 %copy.123 = bf16[256,4096]{0,1:T(8,128)(2,1)} copy(bf16[256,4096]{1,0:T(8,128)(2,1)} %param.13) | data formatting | bytes 4194304 | tf_op args[1]
  61.3 25.7 %all-to-all-done.1 = bf16[256,4,1024]{0,2,1:T(8,128)(2,1)} async-done(((bf16[256,4,1024]{0,2,1:T(8,128)(2,1)}), bf16[256,4,1024]{0,2,1:T(8,128)(2,1)}, u32[]{:S(2)}, u32[]{:S(2)}) %all-to-all-start.1) | async-done | bytes 2097184 | tf_op jit(solution)/shard_map/all_to_all | solution.py:63
  87.1 4.6 %all-to-all-start.3 = ((bf16[256,4,1024]{0,2,1:T(8,128)(2,1)}), bf16[256,4,1024]{0,2,1:T(8,128)(2,1)}, u32[]{:S(2)}, u32[]{:S(2)}) async-start(bf16[256,4,1024]{0,2,1:T(8,128)(2,1)} %bitcast.98), calls=%async_computation.3 | async-start | bytes 4194304 | tf_op jit(solution)/shard_map/all_to_all | solution.py:64
  91.7 0.1 reduce_sum.24
  91.8 0.1 gather.19
  91.9 0.6 dynamic_slice.7
  94.5 0.8 copy.120
  95.3 1.6 gather_fusion.2
  96.9 0.9 convolution_bitcast_fusion
  97.9 2.0 convert_bitcast_fusion.1
  99.8 4.8 %copy.114 = f32[4,256,1024]{1,0,2:T(4,128)} copy(f32[4,256,1024]{1,2,0:T(8,128)S(1)} %convert_bitcast_fusion.1) | data formatting | bytes 8388608 | tf_op jit(solution)/shard_map/convert_element_type | solution.py:69
  104.7 5.8 %reshape.326 = f32[1024,4,256]{0,2,1:T(8,128)} reshape(f32[4,256,1024]{1,0,2:T(4,128)} %copy.114) | data formatting | bytes 8388608 | tf_op jit(solution)/shard_map/convert_element_type | solution.py:69
  110.5 20.1 %all-to-all-done.3 = bf16[256,4,1024]{0,2,1:T(8,128)(2,1)} async-done(((bf16[256,4,1024]{0,2,1:T(8,128)(2,1)}), bf16[256,4,1024]{0,2,1:T(8,128)(2,1)}, u32[]{:S(2)}, u32[]{:S(2)}) %all-to-all-start.3) | async-done | bytes 2097184 | tf_op jit(solution)/shard_map/all_to_all | solution.py:64
  130.6 2.2 convert_bitcast_fusion
  132.8 4.7 %copy.124 = f32[4,256,1024]{1,0,2:T(4,128)} copy(f32[4,256,1024]{1,2,0:T(8,128)S(1)} %convert_bitcast_fusion) | data formatting | bytes 8388608 | tf_op jit(solution)/shard_map/convert_element_type | solution.py:66
  137.4 5.9 %reshape.327 = f32[1024,4,256]{0,2,1:T(8,128)} reshape(f32[4,256,1024]{1,0,2:T(4,128)} %copy.124) | data formatting | bytes 8388608 | tf_op jit(solution)/shard_map/convert_element_type | solution.py:66
  143.3 7.2 %fusion.2 = bf16[1024,4,256]{0,2,1:T(8,128)(2,1)} fusion(f32[1024,4,256]{0,2,1:T(8,128)} %reshape.327, f32[1024,4,256]{0,2,1:T(8,128)} %reshape.326, f32[4,3,256]{2,1,0:T(4,128)S(1)} %convolution_bitcast_fusion, f32[3,1024]{1,0:T(4,128)S(1)} %copy-done.4), kind=kOutput, calls=%fused_computation.8 | convolution fusion | flops 40894464 | bytes 10510336 | tf_op jit(solution)/shard_map/jd,cjt->dct/dot_general | solution.py:67
  150.5 4.3 %copy.125 = bf16[1024,4,256]{2,1,0:T(4,128)(2,1)} copy(bf16[1024,4,256]{0,2,1:T(8,128)(2,1)} %fusion.2) | data formatting | bytes 4194304 | tf_op jit(solution)/shard_map/convert_element_type | solution.py:71
  154.8 4.1 %reshape.321 = bf16[4096,256]{1,0:T(8,128)(2,1)} reshape(bf16[1024,4,256]{2,1,0:T(4,128)(2,1)} %copy.125) | data formatting | bytes 4194304 | tf_op jit(solution)/shard_map/reshape | solution.py:73
  158.9 3.7 %convolution_convert_fusion.1 = bf16[4096,256]{1,0:T(8,128)(2,1)} fusion(bf16[4096,256]{1,0:T(8,128)(2,1)} %reshape.321, bf16[256,256]{1,0:T(8,128)(2,1)S(1)} %copy-done.2), kind=kOutput, calls=%fused_computation.5 | convolution fusion | flops 537919488 | bytes 4325376 | tf_op jit(solution)/shard_map/dot_general | solution.py:72
  162.5 4.4 %reshape.322 = bf16[1024,1024]{1,0:T(8,128)(2,1)} reshape(bf16[4096,256]{1,0:T(8,128)(2,1)} %convolution_convert_fusion.1) | data formatting | bytes 4194304 | tf_op jit(solution)/shard_map/reshape | solution.py:77
  166.9 7.8 %constant_dynamic-slice_fusion = bf16[1,1024,1024]{2,0,1:T(2,128)(2,1)S(1)} fusion(bf16[7,1024,1024]{2,0,1:T(8,128)(2,1)} %all-gather.2.cloned.1.call-done, s32[]{:T(128)S(6)} %select_n.167), kind=kLoop, calls=%fused_computation.81 | loop fusion | bytes 4194308 | tf_op jit(solution)/shard_map/jit(dynamic_index_in_dim)/dynamic_slice | solution.py:59
  174.7 3.7 %fusion.6 = bf16[1024,1024]{1,0:T(8,128)(2,1)} fusion(bf16[1024,1024]{1,0:T(8,128)(2,1)S(1)} %copy-done.1, bf16[1,1024,1024]{2,0,1:T(2,128)(2,1)S(1)} %constant_dynamic-slice_fusion), kind=kOutput, calls=%fused_computation.15 | convolution fusion | flops 2148532224 | bytes 6291456 | tf_op jit(solution)/shard_map/dot_general | solution.py:78
  178.4 4.4 %reshape.323 = bf16[4096,256]{1,0:T(8,128)(2,1)} reshape(bf16[1024,1024]{1,0:T(8,128)(2,1)} %fusion.6) | data formatting | bytes 4194304 | tf_op jit(solution)/shard_map/reshape | solution.py:80
  182.8 4.3 %fusion = f32[4096,256]{1,0:T(8,128)} fusion(bf16[4096,256]{1,0:T(8,128)(2,1)} %reshape.323, bf16[256,256]{1,0:T(8,128)(2,1)S(1)} %copy-done.2), kind=kOutput, calls=%fused_computation.4 | convolution fusion | flops 538968064 | bytes 6422528 | tf_op jit(solution)/shard_map/dot_general | solution.py:79
  187.1 5.2 %reshape.328 = f32[1024,4,256]{2,1,0:T(4,128)} reshape(f32[4096,256]{1,0:T(8,128)} %fusion) | data formatting | bytes 8388608 | tf_op jit(solution)/shard_map/convert_element_type | solution.py:89
  192.3 5.2 %copy.126 = f32[1024,4,256]{0,2,1:T(8,128)} copy(f32[1024,4,256]{2,1,0:T(4,128)} %reshape.328) | data formatting | bytes 8388608 | tf_op jit(solution)/shard_map/convert_element_type | solution.py:89
  197.5 7.2 %fusion.10 = bf16[4,256,3,1]{1,2,3,0:T(4,128)(2,1)S(1)} fusion(f32[1024,4,256]{0,2,1:T(8,128)} %copy.126, f32[1024,4,256]{0,2,1:T(8,128)} %reshape.327, f32[3,1024]{1,0:T(4,128)S(1)} %copy-done.4), kind=kOutput, calls=%fused_computation.18 | convolution fusion | flops 38800384 | bytes 8407040 | tf_op jit(solution)/shard_map/jd,dct->cjt/dot_general | solution.py:86
  204.7 0.5 fusion.35
  205.2 0.4 fusion.13
  205.7 1.1 copy.129
  206.7 6.5 %all-to-all-start.4 = ((f32[64,2,3,256]{3,1,2,0:T(2,128)}), f32[64,2,3,256]{3,1,2,0:T(2,128)S(1)}, u32[]{:S(2)}, u32[]{:S(2)}) async-start(f32[64,2,3,256]{3,1,2,0:T(2,128)} %copy.129), calls=%async_computation.4 | async-start | bytes 786432 | tf_op jit(solution)/shard_map/all_to_all | solution.py:99
  213.2 0.5 broadcast.425
  213.8 2.1 reduce.3
  215.9 0.9 eq.71
  216.7 11.3 %all-to-all-done.4 = f32[64,2,3,256]{3,1,2,0:T(2,128)S(1)} async-done(((f32[64,2,3,256]{3,1,2,0:T(2,128)}), f32[64,2,3,256]{3,1,2,0:T(2,128)S(1)}, u32[]{:S(2)}, u32[]{:S(2)}) %all-to-all-start.4) | async-done | bytes 393248 | tf_op jit(solution)/shard_map/all_to_all | solution.py:99
  228.0 0.1 copy.130
  228.2 0.8 copy.141
  229.0 1.1 copy.131
  230.1 1.0 fusion.21
  231.1 1.6 copy.132
  232.7 40.0 %all-reduce.2.cloned.1.call-done = f32[32,3,256]{2,0,1:T(8,128)} async-done(((f32[32,3,256]{2,0,1:T(8,128)}), f32[32,3,256]{2,0,1:T(8,128)}) %all-reduce.2.cloned.1.call-update) | async-done | bytes 98320 | tf_op jit(solution)/shard_map/psum | solution.py:109
  272.7 2.3 multiply_add_fusion
  (31 shorter events, 0.4 us)
Async XLA Ops:
  7.2 89.8 %copy-start = (bf16[4,6,256,256]{3,2,1,0:T(8,128)(2,1)S(1)}, bf16[4,6,256,256]{3,2,1,0:T(8,128)(2,1)}, u32[]{:S(2)}) copy-start(bf16[4,6,256,256]{3,2,1,0:T(8,128)(2,1)} %param.18) | copy-start | bytes 9437188
  7.2 159.8 %all-gather.2.cloned.1.call-start = ((), (), s32[]{:S(2)}) async-start(), calls=%async_computation.5 | async-start | bytes 16842752 | tf_op jit(solution)/shard_map/all_gather | solution.py:60
  12.9 20.6 %all-to-all-start = ((s32[64,1,2]{2,1,0:T(1,128)}), s32[64,1,2]{2,1,0:T(1,128)S(1)}, u32[]{:S(2)}, u32[]{:S(2)}) async-start(s32[64,1,2]{2,1,0:T(1,128)} %bitcast.2), calls=%async_computation | async-start | bytes 65536 | tf_op jit(solution)/shard_map/all_to_all | solution.py:45
  33.5 0.6 copy-start.3
  35.9 16.9 %all-to-all-start.2 = ((bf16[64,2,3,256]{3,1,2,0:T(2,128)(2,1)}), bf16[64,2,3,256]{3,1,2,0:T(2,128)(2,1)S(1)}, u32[]{:S(2)}, u32[]{:S(2)}) async-start(bf16[64,2,3,256]{3,1,2,0:T(2,128)(2,1)} %broadcast_select_fusion), calls=%async_computation.2 | async-start | bytes 393216 | tf_op jit(solution)/shard_map/all_to_all | solution.py:48
  52.7 34.3 %all-to-all-start.1 = ((bf16[256,4,1024]{0,2,1:T(8,128)(2,1)}), bf16[256,4,1024]{0,2,1:T(8,128)(2,1)}, u32[]{:S(2)}, u32[]{:S(2)}) async-start(bf16[256,4,1024]{0,2,1:T(8,128)(2,1)} %bitcast.99), calls=%async_computation.1 | async-start | bytes 4194304 | tf_op jit(solution)/shard_map/all_to_all | solution.py:63
  61.3 30.6 %copy-start.6 = (s32[64]{0:T(128)S(1)}, s32[64]{0:T(128)}, u32[]{:S(2)}) copy-start(s32[64]{0:T(128)} %param.17) | copy-start | bytes 772
  61.3 33.1 %copy-start.5 = (s32[4,6]{1,0:T(4,128)S(1)}, s32[4,6]{1,0:T(4,128)}, u32[]{:S(2)}) copy-start(s32[4,6]{1,0:T(4,128)} %param.19) | copy-start | bytes 292
  87.1 43.5 %all-to-all-start.3 = ((bf16[256,4,1024]{0,2,1:T(8,128)(2,1)}), bf16[256,4,1024]{0,2,1:T(8,128)(2,1)}, u32[]{:S(2)}, u32[]{:S(2)}) async-start(bf16[256,4,1024]{0,2,1:T(8,128)(2,1)} %bitcast.98), calls=%async_computation.3 | async-start | bytes 4194304 | tf_op jit(solution)/shard_map/all_to_all | solution.py:64
  137.4 5.9 %copy-start.4 = (f32[3,1024]{1,0:T(4,128)S(1)}, f32[3,1024]{1,0:T(4,128)}, u32[]{:S(2)}) copy-start(f32[3,1024]{1,0:T(4,128)} %param.14) | copy-start | bytes 36868
  154.8 4.1 %copy-start.2 = (bf16[256,256]{1,0:T(8,128)(2,1)S(1)}, bf16[256,256]{1,0:T(8,128)(2,1)}, u32[]{:S(2)}) copy-start(bf16[256,256]{1,0:T(8,128)(2,1)} %param.15) | copy-start | bytes 393220
  166.9 7.8 %copy-start.1 = (bf16[1024,1024]{1,0:T(8,128)(2,1)S(1)}, bf16[1024,1024]{1,0:T(8,128)(2,1)}, u32[]{:S(2)}) copy-start(bf16[1024,1024]{1,0:T(8,128)(2,1)} %reshape.322) | copy-start | bytes 6291460
  206.7 21.3 %all-to-all-start.4 = ((f32[64,2,3,256]{3,1,2,0:T(2,128)}), f32[64,2,3,256]{3,1,2,0:T(2,128)S(1)}, u32[]{:S(2)}, u32[]{:S(2)}) async-start(f32[64,2,3,256]{3,1,2,0:T(2,128)} %copy.129), calls=%async_computation.4 | async-start | bytes 786432 | tf_op jit(solution)/shard_map/all_to_all | solution.py:99
  213.2 59.5 %all-reduce.2.cloned.1.call-start = ((), (), s32[]{:S(2)}) async-start(), calls=%async_computation.6 | async-start | bytes 196608 | tf_op jit(solution)/shard_map/psum | solution.py:109
Sparse Core Ops, SparseCore 0:
  12.2 136.2 all-gather.1
  231.3 41.4 all-reduce.1
where the time goes:
time: 284 us; the launch traced here: 282 us
  waiting for transfers between devices  109 us (38%)
  local copies, waits for them, and re-layouts  82.1 us (29%)
  starting transfers between devices  33.1 us (12%)
  matrix products  28.8 us (10%)
  between operations  16.2 us (6%)
  other arithmetic  12.3 us (4%)
    psum x1, waiting for transfers between devices, shards(): summed = lax.psum(owned_sum, 'wafer')  40 us
    all_to_all x1, waiting for transfers between devices, shards(): lax.all_to_all(timestream, 'wafer', split_axis=1, concat_axis=0, tiled=True)  25.7 us
    all_to_all x1, waiting for transfers between devices, shards(): lax.all_to_all(sample_weight, 'wafer', split_axis=1, concat_axis=0, tiled...  20.1 us
    unnamed x19, local copies, waits for them, and re-layouts  12.4 us
    all_to_all x1, starting transfers between devices, shards(): lax.all_to_all(requests, 'tm', split_axis=0, concat_axis=0, tiled=True)  12 us
    all_to_all x1, waiting for transfers between devices, shards(): lax.all_to_all(outgoing, 'tm', split_axis=0, concat_axis=0, tiled=True)  11.3 us
    convert_element_type x2, local copies, waits for them, and re-layouts, shards(): columns.astype(jnp.float32).reshape(det_total, spans_here, samples) - signal  10.7 us
    convert_element_type x2, local copies, waits for them, and re-layouts, shards(): column_weights.astype(jnp.float32).reshape(det_total, spans_here, samples)  10.6 us
  transfers between devices with their start and end apart: 7, of which 6 were waited for; matrix products, arithmetic and copies ran while one was open for 27% of the time, Pallas kernels for 0%

commit v1 on v0

--- a/solution.py
+++ b/solution.py
@@ -2,6 +2,7 @@
 import jax.numpy as jnp
 from jax import lax
 from jax.sharding import PartitionSpec as P
+from jax.lax import all_gather
 
 
 def shards(
@@ -106,7 +107,8 @@
         precision=precise_mode,
     )
     owned_sum = owned_sum.reshape(tiles_own, comp_count, pixel_count)
-    summed = lax.psum(owned_sum, "wafer")
+    current_value = all_gather(owned_sum, axis_name="wafer")
+    summed = jnp.sum(current_value, 0)
     residual_next = summed * float(det_total) ** (-0.5)
     direction_next = residual_next + blend_weight * direction
     return (updated, residual_next, direction_next)

time: 284 us -> 255 us (0.90)
  waiting for transfers between devices: 109 us -> 67.4 us
  blocking collectives: 0 us -> 12.6 us
    psum x1 -> x0, waiting for transfers between devices: 40 us -> none  [shards(): summed = lax.psum(owned_sum, 'wafer')]
    all_gather x0 -> x1, blocking collectives: none -> 12.6 us  [shards(): current_value = all_gather(owned_sum, axis_name='wafer')]
  transfers between devices with their start and end apart: 7 -> 6, of which waited for: 6 -> 5; matrix products, arithmetic and copies ran while one was open for 27% -> 30% of each run, Pallas kernels for 0% -> 0%
where the time goes in v1:
time: 255 us; the launch traced here: 253 us
  local copies, waits for them, and re-layouts  82 us (32%)
  waiting for transfers between devices  67.4 us (26%)
  starting transfers between devices  33.3 us (13%)
  matrix products  28.1 us (11%)
  between operations  16.2 us (6%)
  other arithmetic  13 us (5%)
  blocking collectives  12.6 us (5%)
    all_to_all x1, waiting for transfers between devices, shards(): lax.all_to_all(timestream, 'wafer', split_axis=1, concat_axis=0, tiled=True)  25.7 us
    all_to_all x1, waiting for transfers between devices, shards(): lax.all_to_all(sample_weight, 'wafer', split_axis=1, concat_axis=0, tiled...  19.9 us
    all_gather x1, blocking collectives, shards(): current_value = all_gather(owned_sum, axis_name='wafer')  12.6 us
    unnamed x19, local copies, waits for them, and re-layouts  12.3 us
    all_to_all x1, starting transfers between devices, shards(): lax.all_to_all(requests, 'tm', split_axis=0, concat_axis=0, tiled=True)  12 us
    convert_element_type x2, local copies, waits for them, and re-layouts, shards(): columns.astype(jnp.float32).reshape(det_total, spans_here, samples) - signal  10.7 us
    convert_element_type x2, local copies, waits for them, and re-layouts, shards(): column_weights.astype(jnp.float32).reshape(det_total, spans_here, samples)  10.6 us
    convert_element_type x2, local copies, waits for them, and re-layouts, shards(): smoothed.astype(jnp.float32) * column_weights  10.5 us
  transfers between devices with their start and end apart: 6, of which 5 were waited for; matrix products, arithmetic and copies ran while one was open for 30% of the time, Pallas kernels for 0%

profile of v1, /device:TPU:2, one launch (start us, length us, event | category | flops | bytes accessed | tf_op | source)
XLA Modules:
  0.0 252.6 jit_solution(1439315080975928290)
XLA Ops:
  7.2 1.6 copy.111
  8.9 0.8 reshape.376
  9.6 0.8 reshape.375
  10.4 1.4 gather_fusion
  11.8 0.2 convert_reduce_fusion
  12.0 0.1 select_reduce_fusion
  12.1 0.8 all_to_all.36
  12.9 12.0 %all-to-all-start = ((s32[64,1,2]{2,1,0:T(1,128)}), s32[64,1,2]{2,1,0:T(1,128)S(1)}, u32[]{:S(2)}, u32[]{:S(2)}) async-start(s32[64,1,2]{2,1,0:T(1,128)} %bitcast.2), calls=%async_computation | async-start | bytes 65536 | tf_op jit(solution)/shard_map/all_to_all | solution.py:46
  24.9 1.3 fusion.34
  26.2 2.4 fusion.33
  28.6 4.8 %all-to-all-done = s32[64,1,2]{2,1,0:T(1,128)S(1)} async-done(((s32[64,1,2]{2,1,0:T(1,128)}), s32[64,1,2]{2,1,0:T(1,128)S(1)}, u32[]{:S(2)}, u32[]{:S(2)}) %all-to-all-start) | async-done | bytes 544 | tf_op jit(solution)/shard_map/all_to_all | solution.py:46
  33.5 0.1 copy.116
  33.7 0.1 copy.118
  33.8 0.1 reshape.396
  33.9 0.1 copy-done.3
  34.1 0.8 gather_fusion.1
  34.9 0.9 broadcast_select_fusion
  35.9 5.5 %all-to-all-start.2 = ((bf16[64,2,3,256]{3,1,2,0:T(2,128)(2,1)}), bf16[64,2,3,256]{3,1,2,0:T(2,128)(2,1)S(1)}, u32[]{:S(2)}, u32[]{:S(2)}) async-start(bf16[64,2,3,256]{3,1,2,0:T(2,128)(2,1)} %broadcast_select_fusion), calls=%async_computation.2 | async-start | bytes 393216 | tf_op jit(solution)/shard_map/all_to_all | solution.py:49
  41.4 4.1 %copy.113 = bf16[256,4096]{0,1:T(8,128)(2,1)} copy(bf16[256,4096]{1,0:T(8,128)(2,1)} %param.12) | data formatting | bytes 4194304 | tf_op args[0]
  45.4 7.2 %all-to-all-done.2 = bf16[64,2,3,256]{3,1,2,0:T(2,128)(2,1)S(1)} async-done(((bf16[64,2,3,256]{3,1,2,0:T(2,128)(2,1)}), bf16[64,2,3,256]{3,1,2,0:T(2,128)(2,1)S(1)}, u32[]{:S(2)}, u32[]{:S(2)}) %all-to-all-start.2) | async-done | bytes 196640 | tf_op jit(solution)/shard_map/all_to_all | solution.py:49
  52.7 4.6 %all-to-all-start.1 = ((bf16[256,4,1024]{0,2,1:T(8,128)(2,1)}), bf16[256,4,1024]{0,2,1:T(8,128)(2,1)}, u32[]{:S(2)}, u32[]{:S(2)}) async-start(bf16[256,4,1024]{0,2,1:T(8,128)(2,1)} %bitcast.102), calls=%async_computation.1 | async-start | bytes 4194304 | tf_op jit(solution)/shard_map/all_to_all | solution.py:64
  57.2 4.1 %copy.123 = bf16[256,4096]{0,1:T(8,128)(2,1)} copy(bf16[256,4096]{1,0:T(8,128)(2,1)} %param.13) | data formatting | bytes 4194304 | tf_op args[1]
  61.3 25.7 %all-to-all-done.1 = bf16[256,4,1024]{0,2,1:T(8,128)(2,1)} async-done(((bf16[256,4,1024]{0,2,1:T(8,128)(2,1)}), bf16[256,4,1024]{0,2,1:T(8,128)(2,1)}, u32[]{:S(2)}, u32[]{:S(2)}) %all-to-all-start.1) | async-done | bytes 2097184 | tf_op jit(solution)/shard_map/all_to_all | solution.py:64
  87.1 4.6 %all-to-all-start.3 = ((bf16[256,4,1024]{0,2,1:T(8,128)(2,1)}), bf16[256,4,1024]{0,2,1:T(8,128)(2,1)}, u32[]{:S(2)}, u32[]{:S(2)}) async-start(bf16[256,4,1024]{0,2,1:T(8,128)(2,1)} %bitcast.101), calls=%async_computation.3 | async-start | bytes 4194304 | tf_op jit(solution)/shard_map/all_to_all | solution.py:65
  91.7 0.1 reduce_sum.33
  91.9 0.6 dynamic_slice.7
  94.5 0.8 copy.120
  95.3 1.6 gather_fusion.2
  96.9 0.9 convolution_bitcast_fusion
  97.9 2.0 convert_bitcast_fusion.1
  99.8 4.9 %copy.114 = f32[4,256,1024]{1,0,2:T(4,128)} copy(f32[4,256,1024]{1,2,0:T(8,128)S(1)} %convert_bitcast_fusion.1) | data formatting | bytes 8388608 | tf_op jit(solution)/shard_map/convert_element_type | solution.py:70
  104.8 5.8 %reshape.383 = f32[1024,4,256]{0,2,1:T(8,128)} reshape(f32[4,256,1024]{1,0,2:T(4,128)} %copy.114) | data formatting | bytes 8388608 | tf_op jit(solution)/shard_map/convert_element_type | solution.py:70
  110.6 19.9 %all-to-all-done.3 = bf16[256,4,1024]{0,2,1:T(8,128)(2,1)} async-done(((bf16[256,4,1024]{0,2,1:T(8,128)(2,1)}), bf16[256,4,1024]{0,2,1:T(8,128)(2,1)}, u32[]{:S(2)}, u32[]{:S(2)}) %all-to-all-start.3) | async-done | bytes 2097184 | tf_op jit(solution)/shard_map/all_to_all | solution.py:65
  130.5 2.2 convert_bitcast_fusion
  132.7 4.7 %copy.124 = f32[4,256,1024]{1,0,2:T(4,128)} copy(f32[4,256,1024]{1,2,0:T(8,128)S(1)} %convert_bitcast_fusion) | data formatting | bytes 8388608 | tf_op jit(solution)/shard_map/convert_element_type | solution.py:67
  137.4 5.9 %reshape.384 = f32[1024,4,256]{0,2,1:T(8,128)} reshape(f32[4,256,1024]{1,0,2:T(4,128)} %copy.124) | data formatting | bytes 8388608 | tf_op jit(solution)/shard_map/convert_element_type | solution.py:67
  143.2 7.2 %fusion.2 = bf16[1024,4,256]{0,2,1:T(8,128)(2,1)} fusion(f32[1024,4,256]{0,2,1:T(8,128)} %reshape.384, f32[1024,4,256]{0,2,1:T(8,128)} %reshape.383, f32[4,3,256]{2,1,0:T(4,128)S(1)} %convolution_bitcast_fusion, f32[3,1024]{1,0:T(4,128)S(1)} %copy-done.4), kind=kOutput, calls=%fused_computation.8 | convolution fusion | flops 40894464 | bytes 10510336 | tf_op jit(solution)/shard_map/jd,cjt->dct/dot_general | solution.py:68
  150.4 4.2 %copy.125 = bf16[1024,4,256]{2,1,0:T(4,128)(2,1)} copy(bf16[1024,4,256]{0,2,1:T(8,128)(2,1)} %fusion.2) | data formatting | bytes 4194304 | tf_op jit(solution)/shard_map/convert_element_type | solution.py:72
  154.7 4.0 %reshape.378 = bf16[4096,256]{1,0:T(8,128)(2,1)} reshape(bf16[1024,4,256]{2,1,0:T(4,128)(2,1)} %copy.125) | data formatting | bytes 4194304 | tf_op jit(solution)/shard_map/reshape | solution.py:74
  158.7 3.6 %convolution_convert_fusion.1 = bf16[4096,256]{1,0:T(8,128)(2,1)} fusion(bf16[4096,256]{1,0:T(8,128)(2,1)} %reshape.378, bf16[256,256]{1,0:T(8,128)(2,1)S(1)} %copy-done.2), kind=kOutput, calls=%fused_computation.5 | convolution fusion | flops 537919488 | bytes 4325376 | tf_op jit(solution)/shard_map/dot_general | solution.py:73
  162.3 4.4 %reshape.379 = bf16[1024,1024]{1,0:T(8,128)(2,1)} reshape(bf16[4096,256]{1,0:T(8,128)(2,1)} %convolution_convert_fusion.1) | data formatting | bytes 4194304 | tf_op jit(solution)/shard_map/reshape | solution.py:78
  166.7 7.8 %constant_dynamic-slice_fusion = bf16[1,1024,1024]{2,0,1:T(2,128)(2,1)S(1)} fusion(bf16[7,1024,1024]{2,0,1:T(8,128)(2,1)} %all-gather.3.cloned.1.call-done, s32[]{:T(128)S(6)} %select_n.167), kind=kLoop, calls=%fused_computation.81 | loop fusion | bytes 4194308 | tf_op jit(solution)/shard_map/jit(dynamic_index_in_dim)/dynamic_slice | solution.py:60
  174.5 3.7 %fusion.6 = bf16[1024,1024]{1,0:T(8,128)(2,1)} fusion(bf16[1024,1024]{1,0:T(8,128)(2,1)S(1)} %copy-done.1, bf16[1,1024,1024]{2,0,1:T(2,128)(2,1)S(1)} %constant_dynamic-slice_fusion), kind=kOutput, calls=%fused_computation.15 | convolution fusion | flops 2148532224 | bytes 6291456 | tf_op jit(solution)/shard_map/dot_general | solution.py:79
  178.2 4.3 %reshape.380 = bf16[4096,256]{1,0:T(8,128)(2,1)} reshape(bf16[1024,1024]{1,0:T(8,128)(2,1)} %fusion.6) | data formatting | bytes 4194304 | tf_op jit(solution)/shard_map/reshape | solution.py:81
  182.5 4.3 %fusion = f32[4096,256]{1,0:T(8,128)} fusion(bf16[4096,256]{1,0:T(8,128)(2,1)} %reshape.380, bf16[256,256]{1,0:T(8,128)(2,1)S(1)} %copy-done.2), kind=kOutput, calls=%fused_computation.4 | convolution fusion | flops 538968064 | bytes 6422528 | tf_op jit(solution)/shard_map/dot_general | solution.py:80
  186.8 5.2 %reshape.385 = f32[1024,4,256]{2,1,0:T(4,128)} reshape(f32[4096,256]{1,0:T(8,128)} %fusion) | data formatting | bytes 8388608 | tf_op jit(solution)/shard_map/convert_element_type | solution.py:90
  192.0 5.3 %copy.126 = f32[1024,4,256]{0,2,1:T(8,128)} copy(f32[1024,4,256]{2,1,0:T(4,128)} %reshape.385) | data formatting | bytes 8388608 | tf_op jit(solution)/shard_map/convert_element_type | solution.py:90
  197.2 7.2 %fusion.10 = bf16[4,256,3,1]{1,2,3,0:T(4,128)(2,1)S(1)} fusion(f32[1024,4,256]{0,2,1:T(8,128)} %copy.126, f32[1024,4,256]{0,2,1:T(8,128)} %reshape.384, f32[3,1024]{1,0:T(4,128)S(1)} %copy-done.4), kind=kOutput, calls=%fused_computation.18 | convolution fusion | flops 38800384 | bytes 8407040 | tf_op jit(solution)/shard_map/jd,dct->cjt/dot_general | solution.py:87
  204.4 0.5 fusion.35
  204.9 0.4 fusion.13
  205.4 1.0 copy.129
  206.4 6.5 %all-to-all-start.4 = ((f32[64,2,3,256]{3,1,2,0:T(2,128)}), f32[64,2,3,256]{3,1,2,0:T(2,128)S(1)}, u32[]{:S(2)}, u32[]{:S(2)}) async-start(f32[64,2,3,256]{3,1,2,0:T(2,128)} %copy.129), calls=%async_computation.4 | async-start | bytes 786432 | tf_op jit(solution)/shard_map/all_to_all | solution.py:100
  212.9 1.6 copy.132
  214.5 0.6 broadcast.449
  215.1 2.1 reduce.3
  217.2 0.9 eq.87
  218.1 9.7 %all-to-all-done.4 = f32[64,2,3,256]{3,1,2,0:T(2,128)S(1)} async-done(((f32[64,2,3,256]{3,1,2,0:T(2,128)}), f32[64,2,3,256]{3,1,2,0:T(2,128)S(1)}, u32[]{:S(2)}, u32[]{:S(2)}) %all-to-all-start.4) | async-done | bytes 393248 | tf_op jit(solution)/shard_map/all_to_all | solution.py:100
  227.8 0.1 copy.130
  227.9 0.8 copy.141
  228.7 1.1 copy.131
  229.9 0.3 fusion.21
  230.2 12.6 %all-gather = f32[128,3,256]{2,0,1:T(8,128)S(1)} all-gather(f32[32,3,256]{2,0,1:T(8,128)S(1)} %fusion.21), channel_id=2, replica_groups=mesh['tm'=64,'wafer'=4] {'wafer'}, dimensions={0}, use_global_device_ids=true | all-gather | bytes 491520 | tf_op jit(solution)/shard_map/all_gather | solution.py:110
  242.8 0.7 reduce_sum.35
  243.5 2.3 multiply_add_fusion
  (30 shorter events, 0.4 us)
Async XLA Ops:
  7.2 89.8 %copy-start = (bf16[4,6,256,256]{3,2,1,0:T(8,128)(2,1)S(1)}, bf16[4,6,256,256]{3,2,1,0:T(8,128)(2,1)}, u32[]{:S(2)}) copy-start(bf16[4,6,256,256]{3,2,1,0:T(8,128)(2,1)} %param.18) | copy-start | bytes 9437188
  7.2 159.5 %all-gather.3.cloned.1.call-start = ((), (), s32[]{:S(2)}) async-start(), calls=%async_computation.5 | async-start | bytes 16842752 | tf_op jit(solution)/shard_map/all_gather | solution.py:61
  12.9 20.6 %all-to-all-start = ((s32[64,1,2]{2,1,0:T(1,128)}), s32[64,1,2]{2,1,0:T(1,128)S(1)}, u32[]{:S(2)}, u32[]{:S(2)}) async-start(s32[64,1,2]{2,1,0:T(1,128)} %bitcast.2), calls=%async_computation | async-start | bytes 65536 | tf_op jit(solution)/shard_map/all_to_all | solution.py:46
  33.5 0.6 copy-start.3
  35.9 16.8 %all-to-all-start.2 = ((bf16[64,2,3,256]{3,1,2,0:T(2,128)(2,1)}), bf16[64,2,3,256]{3,1,2,0:T(2,128)(2,1)S(1)}, u32[]{:S(2)}, u32[]{:S(2)}) async-start(bf16[64,2,3,256]{3,1,2,0:T(2,128)(2,1)} %broadcast_select_fusion), calls=%async_computation.2 | async-start | bytes 393216 | tf_op jit(solution)/shard_map/all_to_all | solution.py:49
  52.7 34.4 %all-to-all-start.1 = ((bf16[256,4,1024]{0,2,1:T(8,128)(2,1)}), bf16[256,4,1024]{0,2,1:T(8,128)(2,1)}, u32[]{:S(2)}, u32[]{:S(2)}) async-start(bf16[256,4,1024]{0,2,1:T(8,128)(2,1)} %bitcast.102), calls=%async_computation.1 | async-start | bytes 4194304 | tf_op jit(solution)/shard_map/all_to_all | solution.py:64
  61.3 30.6 %copy-start.6 = (s32[64]{0:T(128)S(1)}, s32[64]{0:T(128)}, u32[]{:S(2)}) copy-start(s32[64]{0:T(128)} %param.17) | copy-start | bytes 772
  61.3 33.2 %copy-start.5 = (s32[4,6]{1,0:T(4,128)S(1)}, s32[4,6]{1,0:T(4,128)}, u32[]{:S(2)}) copy-start(s32[4,6]{1,0:T(4,128)} %param.19) | copy-start | bytes 292
  87.1 43.4 %all-to-all-start.3 = ((bf16[256,4,1024]{0,2,1:T(8,128)(2,1)}), bf16[256,4,1024]{0,2,1:T(8,128)(2,1)}, u32[]{:S(2)}, u32[]{:S(2)}) async-start(bf16[256,4,1024]{0,2,1:T(8,128)(2,1)} %bitcast.101), calls=%async_computation.3 | async-start | bytes 4194304 | tf_op jit(solution)/shard_map/all_to_all | solution.py:65
  137.4 5.9 %copy-start.4 = (f32[3,1024]{1,0:T(4,128)S(1)}, f32[3,1024]{1,0:T(4,128)}, u32[]{:S(2)}) copy-start(f32[3,1024]{1,0:T(4,128)} %param.14) | copy-start | bytes 36868
  154.6 4.0 %copy-start.2 = (bf16[256,256]{1,0:T(8,128)(2,1)S(1)}, bf16[256,256]{1,0:T(8,128)(2,1)}, u32[]{:S(2)}) copy-start(bf16[256,256]{1,0:T(8,128)(2,1)} %param.15) | copy-start | bytes 393220
  166.7 7.8 %copy-start.1 = (bf16[1024,1024]{1,0:T(8,128)(2,1)S(1)}, bf16[1024,1024]{1,0:T(8,128)(2,1)}, u32[]{:S(2)}) copy-start(bf16[1024,1024]{1,0:T(8,128)(2,1)} %reshape.379) | copy-start | bytes 6291460
  206.4 21.4 %all-to-all-start.4 = ((f32[64,2,3,256]{3,1,2,0:T(2,128)}), f32[64,2,3,256]{3,1,2,0:T(2,128)S(1)}, u32[]{:S(2)}, u32[]{:S(2)}) async-start(f32[64,2,3,256]{3,1,2,0:T(2,128)} %copy.129), calls=%async_computation.4 | async-start | bytes 786432 | tf_op jit(solution)/shard_map/all_to_all | solution.py:100
Sparse Core Ops, SparseCore 0:
  12.2 136.2 all-gather.2
